TPU v7x, 32 devices: a whole 2x2x4 slice. The times are simulated.
32 devices in a mesh: vis: 8 (over y, x, core), tile: 4 (over z).
Axes of the slice: x: 2, y: 2, z: 4, core: 2. Of those that a mesh axis runs over, the one named last changes fastest.
Arguments:
- image: float32 [8192, 8192], P('vis', 'tile'), may hold values from 0 to 2
- extrapolated: float32 [8192, 8192], P('vis', 'tile'), may hold values from -6 to 6
- vis_dual: float32 [8192, 2, 128], P(('vis', 'tile')), may hold values from -6 to 6
- tree_dual: float32 [2, 8192, 4096], P(None, 'vis', 'tile'), may hold values from -6 to 6
- observed: float32 [8192, 2, 128], P(('vis', 'tile')), may hold values from -6 to 6
- kernel: float32 [128, 128], replicated, may hold values from -0.5 to 0.5
- block_index: int32 [8192], P(('vis', 'tile')), may hold values from 0 to 16383
- live_blocks: int32 [32], P(('vis', 'tile')), may hold values from 1 to 256, as said below
Outputs:
- image_next: float32 [8192, 8192], P('vis', 'tile')
- vis_next: float32 [8192, 2, 128], P(('vis', 'tile'))
- tree_next: float32 [2, 8192, 4096], P(None, 'vis', 'tile')
Inputs may be any that keep to these rules, and one draw needn't show every extreme that they name: Each device's live slots are its first live_blocks entries of 256; some device has all 256 live in every draw.
All inputs are finite; a program needn't handle non-finite values.
Results may differ from a plain program's by a relative error of at most 0.00005.
Values sent between devices are 32-bit elements; how exact they have to be, the bound alone decides.
No kernel may reach another device: no remote copies, remote signals or barrier semaphores. Data moves between devices by JAX's collectives and lax.ppermute only.
A program may use at most 192 MiB of HBM per device.

v0:
```python
import math
import jax
import jax.numpy as jnp
from jax import lax
from jax.sharding import PartitionSpec as P

LOW_TAPS = (
    -0.010597401784997278,
    0.032883011666982945,
    0.030841381835986965,
    -0.18703481171888114,
    -0.02798376941698385,
    0.6308807679295904,
    0.7148465705525415,
    0.23037781330885523,
)
HIGH_TAPS = tuple(
    ((1.0 if position % 2 == 0 else -1.0) * LOW_TAPS[7 - position] for position in range(8))
)
TWO_PI = 2.0 * math.pi


def shifted(block, axis, distance):
    devices = range(lax.axis_size(axis))
    route = [((i - distance) % len(devices), i) for i in devices]
    return lax.ppermute(block, axis, route)


def phase_table(left_ids, right_ids, period):
    turns = left_ids[:, None] * right_ids[None, :] % period
    angles = turns.astype(jnp.float32) * (TWO_PI / period)
    return (jnp.cos(angles), jnp.sin(angles))


def factor_pair(length):
    chosen_factor = 1
    for candidate in range(1, math.isqrt(length) + 1):
        if length % candidate == 0:
            chosen_factor = candidate
    return (chosen_factor, length // chosen_factor)


def complex_einsum(form, left_real, left_imag, table_cos, table_sin, real_only):
    precise = lax.Precision.HIGHEST
    real_part = jnp.einsum(form, left_real, table_cos, precision=precise)
    if left_imag is not None:
        real_part = real_part - jnp.einsum(form, left_imag, table_sin, precision=precise)
    if real_only:
        return (real_part, None)
    imag_part = jnp.einsum(form, left_real, table_sin, precision=precise)
    if left_imag is not None:
        imag_part = imag_part + jnp.einsum(form, left_imag, table_cos, precision=precise)
    return (imag_part * 0.0 + real_part, imag_part)


def transform_axis(real_in, imag_in, sign_value, along, real_only):
    length = real_in.shape[along]
    first_factor, second_factor = factor_pair(length)
    first_ids = jnp.arange(first_factor, dtype=jnp.int32)
    second_ids = jnp.arange(second_factor, dtype=jnp.int32)
    cos_first, sin_first = phase_table(first_ids, first_ids, first_factor)
    cos_twist, sin_twist = phase_table(first_ids, second_ids, length)
    cos_second, sin_second = phase_table(second_ids, second_ids, second_factor)
    sin_twist = sign_value * sin_twist
    if along == 0:
        other_len = real_in.shape[1]
        shape_in = (first_factor, second_factor, other_len)
        form_first = "abm,ca->cbm"
        form_second = "cbm,db->dcm"
        cos_twist = cos_twist[:, :, None]
        sin_twist = sin_twist[:, :, None]
        shape_out = (length, other_len)
    else:
        other_len = real_in.shape[0]
        shape_in = (other_len, first_factor, second_factor)
        form_first = "mab,ca->mcb"
        form_second = "mcb,db->mdc"
        cos_twist = cos_twist[None, :, :]
        sin_twist = sin_twist[None, :, :]
        shape_out = (other_len, length)
    shaped_real = real_in.reshape(shape_in)
    shaped_imag = None if imag_in is None else imag_in.reshape(shape_in)
    section_real, section_imag = complex_einsum(
        form_first, shaped_real, shaped_imag, cos_first, sign_value * sin_first, False
    )
    twisted_real = section_real * cos_twist - section_imag * sin_twist
    twisted_imag = section_real * sin_twist + section_imag * cos_twist
    out_real, out_imag = complex_einsum(
        form_second, twisted_real, twisted_imag, cos_second, sign_value * sin_second, real_only
    )
    if real_only:
        return (out_real.reshape(shape_out), None)
    return (out_real.reshape(shape_out), out_imag.reshape(shape_out))


def analyse_local(coarse):
    half_rows = coarse.shape[1] // 2
    next_rows = shifted(coarse[:, :6], "tile", -1)
    extended = jnp.concatenate([coarse, next_rows], axis=1)
    phases = [lax.slice_in_dim(extended, parity, extended.shape[1], 2, 1) for parity in range(2)]
    approx = jnp.zeros((coarse.shape[0], half_rows), jnp.float32)
    detail = jnp.zeros_like(approx)
    for position in range(8):
        strided = lax.slice_in_dim(
            phases[position % 2], position // 2, position // 2 + half_rows, 1, 1
        )
        approx = approx + LOW_TAPS[position] * strided
        detail = detail + HIGH_TAPS[position] * strided
    return (approx, detail)


def upsample(ext_approx, ext_detail):
    out_rows = ext_detail.shape[1] - 3
    even_part = jnp.zeros((ext_detail.shape[0], out_rows), jnp.float32)
    odd_part = jnp.zeros_like(even_part)
    for lag_index in range(4):
        window_detail = ext_detail[:, 3 - lag_index : 3 - lag_index + out_rows]
        even_part = even_part + HIGH_TAPS[2 * lag_index] * window_detail
        odd_part = odd_part + HIGH_TAPS[2 * lag_index + 1] * window_detail
        if ext_approx is not None:
            window_approx = ext_approx[:, 3 - lag_index : 3 - lag_index + out_rows]
            even_part = even_part + LOW_TAPS[2 * lag_index] * window_approx
            odd_part = odd_part + LOW_TAPS[2 * lag_index + 1] * window_approx
    return jnp.stack([even_part, odd_part], axis=2).reshape(ext_detail.shape[0], 2 * out_rows)


def split_three(values):
    first = lax.reduce_precision(values, exponent_bits=8, mantissa_bits=7)
    rest = values - first
    second = lax.reduce_precision(rest, exponent_bits=8, mantissa_bits=7)
    third = rest - second
    pieces = [first, second, third]
    return jnp.concatenate([piece.astype(jnp.bfloat16) for piece in pieces], axis=-1)


def pick_rows(index, table):
    width = table.shape[1]
    selector = (index[:, None] == jnp.arange(table.shape[0], dtype=jnp.int32)[None, :]).astype(
        jnp.bfloat16
    )
    summed = jnp.dot(selector, split_three(table), preferred_element_type=jnp.float32)
    return summed[:, :width] + summed[:, width : 2 * width] + summed[:, 2 * width :]


def rows_to_grid(local_rows, values, row_count):
    groups, members, width = values.shape
    pieces = split_three(values)
    selector = (
        jnp.arange(row_count, dtype=jnp.int32)[None, :, None] == local_rows[:, None, :]
    ).astype(jnp.bfloat16)
    summed = jnp.einsum("gkb,gbc->gkc", selector, pieces, preferred_element_type=jnp.float32)
    summed = summed[..., :width] + summed[..., width : 2 * width] + summed[..., 2 * width :]
    return summed.reshape(groups * row_count, width)


def on_device(image, extrapolated, vis_dual, tree_dual, observed, kernel, block_index, live_blocks):
    precise = lax.Precision.HIGHEST
    slab_rows, slab_cols = image.shape
    n_vis = lax.axis_size("vis")
    n_tile = lax.axis_size("tile")
    vis_id = lax.axis_index("vis")
    tile_id = lax.axis_index("tile")
    len_rows = slab_rows * n_vis
    len_cols = slab_cols * n_tile
    block_width = kernel.shape[0]
    chunk = slab_cols // n_vis
    slot_count = vis_dual.shape[0]
    norm_scale = 1.0 / math.sqrt(len_rows * len_cols)
    columns = lax.all_to_all(extrapolated, "vis", split_axis=1, concat_axis=0, tiled=True)
    spec_real, spec_imag = transform_axis(columns, None, -1.0, 0, False)
    all_index = lax.all_gather(block_index, ("vis", "tile"), tiled=True)
    total_blocks = all_index.shape[0]
    owner = jnp.arange(total_blocks, dtype=jnp.int32) // slot_count
    per_row = slab_cols // block_width
    local_row = all_index // per_row
    row_of = owner // n_tile * slab_rows + local_row
    band_of = owner % n_tile * per_row + all_index % per_row
    col_ids = tile_id * slab_cols + vis_id * chunk + jnp.arange(chunk, dtype=jnp.int32)
    band_count = len_cols // block_width
    band_turns = (
        (jnp.arange(band_count, dtype=jnp.int32) * block_width)[:, None]
        * col_ids[None, :]
        % len_cols
    )
    band_angles = band_turns.astype(jnp.float32) * (TWO_PI / len_cols)
    band_both = pick_rows(band_of, jnp.concatenate([jnp.cos(band_angles), jnp.sin(band_angles)], 1))
    band_cos = band_both[:, :chunk]
    band_sin = band_both[:, chunk:]
    cell_turns = col_ids[:, None] * jnp.arange(block_width, dtype=jnp.int32)[None, :] % len_cols
    cell_angles = cell_turns.astype(jnp.float32) * (TWO_PI / len_cols)
    cell_cos = jnp.cos(cell_angles)
    cell_sin = jnp.sin(cell_angles)
    picked_real = jnp.take(spec_real, row_of, axis=0)
    picked_imag = jnp.take(spec_imag, row_of, axis=0)
    twisted_real = picked_real * band_cos + picked_imag * band_sin
    twisted_imag = picked_imag * band_cos - picked_real * band_sin
    part_real = jnp.dot(twisted_real, cell_cos, precision=precise) + jnp.dot(
        twisted_imag, cell_sin, precision=precise
    )
    part_imag = jnp.dot(twisted_imag, cell_cos, precision=precise) - jnp.dot(
        twisted_real, cell_sin, precision=precise
    )
    partial = jnp.stack([part_real, part_imag], axis=1)
    partial = lax.all_to_all(partial, "vis", split_axis=0, concat_axis=0, tiled=True)
    partial = partial.reshape((n_vis, total_blocks // n_vis) + partial.shape[1:]).sum(axis=0)
    partial = lax.all_to_all(partial, "tile", split_axis=0, concat_axis=0, tiled=True)
    chosen = partial.reshape((n_tile, slot_count) + partial.shape[1:]).sum(axis=0) * norm_scale
    model = jnp.einsum("ij,csj->csi", kernel, chosen, precision=precise)
    live_mask = (jnp.arange(slot_count, dtype=jnp.int32) < live_blocks[0]).astype(jnp.float32)[
        :, None, None
    ]
    misfit = (vis_dual / 0.5 + model - observed) * live_mask
    totals = lax.psum((jnp.sum(misfit * misfit), jnp.sum(live_mask)), ("vis", "tile"))
    radius = jnp.sqrt(2.0 * block_width * totals[1])
    size_now = jnp.sqrt(totals[0])
    vis_next = 0.5 * misfit * (1.0 - radius / jnp.maximum(size_now, radius))
    contrib = jnp.einsum("ij,csi->csj", kernel, vis_next, precision=precise)
    every = lax.all_gather(contrib, "tile", tiled=True)
    every = lax.all_gather(every, "vis", tiled=True)
    back_real = jnp.dot(every[:, 0, :], cell_cos.T, precision=precise) - jnp.dot(
        every[:, 1, :], cell_sin.T, precision=precise
    )
    back_imag = jnp.dot(every[:, 0, :], cell_sin.T, precision=precise) + jnp.dot(
        every[:, 1, :], cell_cos.T, precision=precise
    )
    turned_real = back_real * band_cos - back_imag * band_sin
    turned_imag = back_real * band_sin + back_imag * band_cos
    turned = jnp.concatenate([turned_real, turned_imag], axis=1)
    turned = turned.reshape(n_vis, total_blocks // n_vis, 2 * chunk)
    gridded = rows_to_grid(local_row.reshape(n_vis, total_blocks // n_vis), turned, slab_rows)
    pixel_real, unused_part = transform_axis(gridded[:, :chunk], gridded[:, chunk:], 1.0, 0, True)
    data_term = (
        lax.all_to_all(pixel_real, "vis", split_axis=0, concat_axis=1, tiled=True) * norm_scale
    )
    approx_one, detail_one = analyse_local(extrapolated)
    approx_two, detail_two = analyse_local(approx_one)
    child = tree_dual[0] + 0.5 * detail_one
    parent = tree_dual[1] + 0.5 * jnp.repeat(detail_two, 2, axis=1)
    factor = 1.0 / jnp.maximum(jnp.sqrt(child * child + parent * parent), 1.0)
    child_next = child * factor
    parent_next = parent * factor
    parent_sum = parent_next[:, 0::2] + parent_next[:, 1::2]
    parent_tail = shifted(parent_sum[:, -3:], "tile", 1)
    level_one = upsample(None, jnp.concatenate([parent_tail, parent_sum], axis=1))
    both_tails = shifted(jnp.stack([level_one[:, -3:], child_next[:, -3:]]), "tile", 1)
    prior_term = upsample(
        jnp.concatenate([both_tails[0], level_one], axis=1),
        jnp.concatenate([both_tails[1], child_next], axis=1),
    )
    image_next = jnp.maximum(image - 0.5 * (data_term + prior_term), 0.0)
    return (image_next, vis_next, jnp.stack([child_next, parent_next]))


def solution(mesh):
    return jax.shard_map(
        on_device,
        mesh=mesh,
        in_specs=(
            P("vis", "tile"),
            P("vis", "tile"),
            P(("vis", "tile"), None, None),
            P(None, "vis", "tile"),
            P(("vis", "tile"), None, None),
            P(),
            P(("vis", "tile")),
            P(("vis", "tile")),
        ),
        out_specs=(P("vis", "tile"), P(("vis", "tile"), None, None), P(None, "vis", "tile")),
        check_vma=False,
    )
```

profile of v0, /device:TPU:0, one launch (start us, length us, event | category | flops | bytes accessed | tf_op | source)
XLA Modules:
  0.0 1235.9 jit_solution(12371021110578368048)
XLA Ops:
  21.8 70.9 %all-gather = s32[32,1,256]{2,1,0:T(1,128)S(1)} all-gather(s32[1,1,256]{2,1,0:T(1,128)S(1)} %bitcast.146), channel_id=1, replica_groups=mesh['vis'=8,'tile'=4] {'vis','tile'}, dimensions={0}, use_global_device_ids=true | all-gather | bytes 33792 | tf_op jit(solution)/shard_map/all_gather | solution.py:171
  94.1 19.4 %fusion.63 = f32[8192,1536]{0,1:T(8,128)} fusion(s32[8192]{0:T(1024)S(1)} %fusion.124, bf16[64,512]{1,0:T(8,128)(2,1)S(1)} %get-tuple-element.55, bf16[64,512]{1,0:T(8,128)(2,1)S(1)} %get-tuple-element.54, bf16[64,512]{1,0:T(8,128)(2,1)S(1)} %get-tuple-element.53), kind=kOutput, calls=%fused_computation.120 | convolution fusion | flops 1611726848 | bytes 50561024 | tf_op jit(solution)/shard_map/dot_general | solution.py:141
  113.5 22.7 %slice_add_fusion.2 = f32[8192,512]{0,1:T(8,128)} fusion(f32[8192,1536]{0,1:T(8,128)} %fusion.63), kind=kLoop, calls=%fused_computation.16 | loop fusion | flops 8388608 | bytes 67108864 | tf_op jit(solution)/shard_map/add | solution.py:142
  145.4 17.5 %fusion.33 = f32[64,128,256]{2,0,1:T(8,128)} fusion(f32[64,128,256]{2,1,0:T(8,128)} %bitcast.127), kind=kOutput, calls=%fused_computation.66 | convolution fusion | flops 1610670080 | bytes 16777216 | tf_op jit(solution)/shard_map/abm,ca->cbm/dot_general | solution.py:45
  162.9 18.6 %multiply_subtract_fusion.3 = (f32[64,128,256]{2,0,1:T(8,128)S(1)}, f32[64,128,256]{2,0,1:T(8,128)}) fusion(f32[64,128,256]{2,0,1:T(8,128)} %fusion.33, f32[64,128]{0,1:T(8,128)S(1)} %get-tuple-element.64, f32[64,128]{0,1:T(8,128)S(1)} %get-tuple-element.65, f32[64,128,256]{2,1,0:T(8,128)} %bitcast.128), kind=kOutput, calls=%fused_computation.48 | convolution fusion | flops 1627451392 | bytes 33619968 | tf_op jit(solution)/shard_map/abm,ca->cbm/dot_general | solution.py:50
  181.5 17.5 %fusion.27 = f32[128,64,256]{2,0,1:T(8,128)} fusion(f32[64,128,256]{2,0,1:T(8,128)} %get-tuple-element.41), kind=kOutput, calls=%fused_computation.60 | convolution fusion | flops 3221454848 | bytes 16777216 | tf_op jit(solution)/shard_map/cbm,db->dcm/dot_general | solution.py:52
  199.0 13.5 %fusion.25 = f32[128,64,256]{2,0,1:T(8,128)} fusion(f32[64,128,256]{2,0,1:T(8,128)S(1)} %bitcast.130), kind=kOutput, calls=%fused_computation.58 | convolution fusion | flops 3221471232 | bytes 16777216 | tf_op jit(solution)/shard_map/cbm,db->dcm/dot_general | solution.py:47
  212.5 14.3 %fusion.45 = f32[128,64,256]{2,0,1:T(8,128)S(1)} fusion(f32[128,64,256]{2,0,1:T(8,128)} %fusion.27, f32[64,128,256]{2,0,1:T(8,128)S(1)} %get-tuple-element.40), kind=kOutput, calls=%fused_computation.94 | convolution fusion | flops 3223568384 | bytes 25165824 | tf_op jit(solution)/shard_map/cbm,db->dcm/dot_general | solution.py:50
  235.1 17.4 %subtract_add_fusion.1 = f32[128,64,256]{2,0,1:T(8,128)} fusion(f32[128,64,256]{2,0,1:T(8,128)} %fusion.25, f32[128,64,256]{2,0,1:T(8,128)S(1)} %fusion.45, f32[64,128,256]{2,0,1:T(8,128)S(1)} %get-tuple-element.40), kind=kOutput, calls=%fused_computation.46 | convolution fusion | flops 3227746304 | bytes 33554432 | tf_op jit(solution)/shard_map/cbm,db->dcm/dot_general | solution.py:45
  252.5 11.5 copy.247
  264.0 34.7 %gather_fusion = f32[8192,256]{1,0:T(8,128)} fusion(f32[8192,256]{1,0:T(8,128)} %bitcast.121, s32[8192]{0:T(1024)S(1)} %broadcast_clamp_fusion), kind=kCustom, calls=%fused_computation.clone | custom fusion | bytes 16809984 | tf_op jit(solution)/shard_map/jit(_take)/gather | solution.py:193
  307.6 34.7 %gather_fusion.1 = f32[8192,256]{1,0:T(8,128)} fusion(f32[8192,256]{1,0:T(8,128)} %bitcast.120, s32[8192]{0:T(1024)S(1)} %broadcast_clamp_fusion), kind=kCustom, calls=%fused_computation.1.clone | custom fusion | bytes 16809984 | tf_op jit(solution)/shard_map/jit(_take)/gather | solution.py:194
  351.3 19.2 %multiply_add_fusion.2 = (f32[8192,256]{0,1:T(8,128)}, f32[8192,256]{0,1:T(8,128)}) fusion(f32[8192,256]{0,1:T(8,128)} %copy.250, f32[8192,256]{0,1:T(8,128)} %copy.248, f32[8192,512]{0,1:T(8,128)} %slice_add_fusion.2, pred[8192]{0:T(1024)(128)(4,1)S(1)} %get-tuple-element.30), kind=kLoop, calls=%fused_computation.45 | loop fusion | flops 16777216 | bytes 50339840 | tf_op jit(solution)/shard_map/add | solution.py:195
  370.5 17.2 %fusion.104 = f32[8192,128]{1,0:T(8,128)S(1)} fusion(f32[8192,256]{0,1:T(8,128)} %get-tuple-element.36, s32[256]{0:T(256)S(1)} %copy-done.16), kind=kOutput, calls=%fused_computation.183 | convolution fusion | flops 3221684224 | bytes 12583936 | tf_op jit(solution)/shard_map/dot_general | solution.py:197
  387.8 14.6 %fusion.102 = f32[8192,128]{1,0:T(8,128)S(1)} fusion(f32[8192,256]{0,1:T(8,128)S(1)} %copy-done.2, s32[256]{0:T(256)S(1)} %copy-done.16), kind=kOutput, calls=%fused_computation.182 | convolution fusion | flops 3221684224 | bytes 12583936 | tf_op jit(solution)/shard_map/dot_general | solution.py:200
  402.4 14.8 %fusion.9 = f32[8192,1,128]{2,0,1:T(8,128)S(1)} fusion(f32[8192,128]{1,0:T(8,128)S(1)} %fusion.104, f32[8192,256]{0,1:T(8,128)S(1)} %copy-done.2, s32[256]{0:T(256)S(1)} %copy-done.16), kind=kOutput, calls=%fused_computation.25 | convolution fusion | flops 3222732800 | bytes 16778240 | tf_op jit(solution)/shard_map/dot_general | solution.py:197
  417.2 14.6 %fusion.8 = f32[8192,1,128]{2,0,1:T(8,128)S(1)} fusion(f32[8192,128]{1,0:T(8,128)S(1)} %fusion.102, f32[8192,256]{0,1:T(8,128)S(1)} %bitcast.123, s32[256]{0:T(256)S(1)} %copy-done.16), kind=kOutput, calls=%fused_computation.23 | convolution fusion | flops 3222732800 | bytes 16778240 | tf_op jit(solution)/shard_map/dot_general | solution.py:200
  432.3 31.2 %copy.251 = f32[8192,2,128]{2,1,0:T(2,128)S(1)} copy(f32[8192,2,128]{2,0,1:T(8,128)S(1)} %pad_maximum_fusion.2) | data formatting | bytes 16777216 | tf_op jit(solution)/shard_map/stack | solution.py:203
  463.5 97.4 %all_to_all.39 = f32[8192,2,128]{2,1,0:T(2,128)} all-to-all(f32[8192,2,128]{2,1,0:T(2,128)S(1)} %copy.251), channel_id=1, replica_groups=mesh['vis'=8,'tile'=4] {'vis'}, dimensions={0} | all-to-all | bytes 16777216 | tf_op jit(solution)/shard_map/all_to_all | solution.py:204
  573.2 24.1 %all-to-all-done.2 = f32[1024,2,128]{2,1,0:T(2,128)S(1)} async-done(((f32[1024,2,128]{2,1,0:T(2,128)}), f32[1024,2,128]{2,1,0:T(2,128)S(1)}, u32[]{:S(2)}, u32[]{:S(2)}) %all-to-all-start.2) | async-done | bytes 1048608 | tf_op jit(solution)/shard_map/all_to_all | solution.py:206
  598.9 37.5 %all-reduce = (f32[]{:T(128)}, f32[]{:T(128)}) all-reduce(f32[]{:T(128)} %fusion.168, f32[]{:T(128)} %get-tuple-element.60), channel_id=1, replica_groups=mesh['vis'=8,'tile'=4] {'vis','tile'}, use_global_device_ids=true, to_apply=%region_3.5 | all-reduce | flops 2 | bytes 16 | tf_op jit(solution)/shard_map/psum | solution.py:213
  639.7 29.3 %all-gather.4.cloned.1.call-done = f32[1024,2,128]{2,0,1:T(8,128)} async-done(((f32[256,2,128]{2,0,1:T(8,128)}), f32[1024,2,128]{2,0,1:T(8,128)}) %all-gather.4.cloned.1.call-update) | async-done | bytes 1048592 | tf_op jit(solution)/shard_map/all_gather | solution.py:218
  684.5 18.9 %slice.172 = f32[1024,1027]{0,1:T(8,128)} slice(f32[1024,2054]{0,1:T(8,128)} %pad_maximum_fusion.1), slice={[0:1024:1], [0:2054:2]} | slice | bytes 8413184 | tf_op jit(solution)/shard_map/slice | solution.py:100
  703.4 18.8 %slice.174 = f32[1024,1027]{0,1:T(8,128)} slice(f32[1024,2054]{0,1:T(8,128)} %pad_maximum_fusion.1), slice={[0:1024:1], [1:2054:2]} | slice | bytes 8413184 | tf_op jit(solution)/shard_map/slice | solution.py:100
  722.2 13.6 %multiply_add_fusion.5 = f32[1024,1024]{0,1:T(8,128)S(1)} fusion(f32[1024,1027]{0,1:T(8,128)} %slice.174, f32[1024,1027]{0,1:T(8,128)} %slice.172), kind=kLoop, calls=%fused_computation.91 | loop fusion | flops 15728640 | bytes 37748736 | tf_op jit(solution)/shard_map/add | solution.py:107
  755.9 10.1 slice.184
  765.9 10.1 slice.186
  776.0 10.0 fusion.44
  786.0 10.1 fusion.43
  796.0 10.6 convolution_subtract_fusion
  806.6 22.0 %multiply_subtract_fusion.1 = (f32[8192,256]{0,1:T(8,128)}, f32[8192,256]{0,1:T(8,128)}) fusion(f32[8192,256]{0,1:T(8,128)} %convolution_subtract_fusion, f32[8192,512]{0,1:T(8,128)} %slice_add_fusion.2, f32[8192,256]{0,1:T(8,128)} %fusion.43, s32[256]{0:T(256)S(1)} %copy-done.16, f32[8192,2,128]{2,0,1:T(8,128)} %all-gather.6.cloned.1.call-done), kind=kOutput, calls=%fused_computation.43 | convolution fusion | flops 3236364288 | bytes 54526976 | tf_op jit(solution)/shard_map/dot_general | solution.py:223
  828.6 11.7 pad_maximum_fusion
  840.3 17.5 %copy.276 = f32[8192,512]{1,0:T(8,128)} copy(f32[8192,512]{0,1:T(8,128)} %pad_maximum_fusion) | data formatting | bytes 33554432 | tf_op jit(solution)/shard_map/reshape | solution.py:229
  857.8 10.4 reduce-precision_convert_fusion.1
  868.2 31.5 %fusion = f32[8,1024,1536]{2,1,0:T(8,128)} fusion(bf16[8,1024,512]{2,1,0:T(8,128)(2,1)S(1)} %get-tuple-element.45, bf16[8,1024,512]{2,1,0:T(8,128)(2,1)} %get-tuple-element.46, bf16[8,1024,512]{2,1,0:T(8,128)(2,1)S(1)} %get-tuple-element.44, s32[8,1024]{1,0:T(8,128)S(1)} %eq.45), kind=kOutput, calls=%fused_computation.3 | convolution fusion | flops 25853689856 | bytes 75530240 | tf_op jit(solution)/shard_map/gkb,gbc->gkc/dot_general | solution.py:151
  899.7 23.9 %slice_add_fusion = f32[8,1024,512]{2,1,0:T(8,128)} fusion(f32[8,1024,1536]{2,1,0:T(8,128)} %fusion), kind=kLoop, calls=%fused_computation.14 | loop fusion | flops 8388608 | bytes 67108864 | tf_op jit(solution)/shard_map/add | solution.py:152
  930.0 13.2 %fusion.17 = f32[64,128,256]{2,0,1:T(8,128)} fusion(f32[64,128,256]{2,1,0:T(8,128)S(1)} %bitcast.131), kind=kOutput, calls=%fused_computation.50 | convolution fusion | flops 1610670080 | bytes 16777216 | tf_op jit(solution)/shard_map/abm,ca->cbm/dot_general | solution.py:47
  943.2 13.6 %fusion.19 = f32[64,128,256]{2,0,1:T(8,128)} fusion(f32[64,128,256]{2,1,0:T(8,128)S(1)} %bitcast.132), kind=kOutput, calls=%fused_computation.52 | convolution fusion | flops 1610670080 | bytes 16777216 | tf_op jit(solution)/shard_map/abm,ca->cbm/dot_general | solution.py:52
  956.8 13.2 %fusion.23 = f32[64,128,256]{2,0,1:T(8,128)} fusion(f32[64,128,256]{2,1,0:T(8,128)S(1)} %bitcast.133), kind=kOutput, calls=%fused_computation.56 | convolution fusion | flops 1610670080 | bytes 16777216 | tf_op jit(solution)/shard_map/abm,ca->cbm/dot_general | solution.py:50
  969.9 21.5 %multiply_subtract_fusion = (f32[64,128,256]{2,0,1:T(8,128)}, f32[64,128,256]{2,0,1:T(8,128)}) fusion(f32[64,128,256]{2,0,1:T(8,128)} %fusion.17, f32[64,128]{0,1:T(8,128)S(1)} %copy-done.12, f32[64,128]{0,1:T(8,128)S(1)} %copy-done.9, f32[64,128,256]{2,0,1:T(8,128)} %fusion.23, f32[64,128,256]{2,0,1:T(8,128)} %fusion.19, f32[64,128,256]{2,1,0:T(8,128)S(1)} %bitcast.134), kind=kOutput, calls=%fused_computation.40 | convolution fusion | flops 1631641600 | bytes 50397184 | tf_op jit(solution)/shard_map/abm,ca->cbm/dot_general | solution.py:45
  991.5 16.3 %fusion.13 = f32[128,64,256]{2,0,1:T(8,128)S(1)} fusion(f32[64,128,256]{2,0,1:T(8,128)} %get-tuple-element.35), kind=kOutput, calls=%fused_computation.34 | convolution fusion | flops 3221454848 | bytes 16777216 | tf_op jit(solution)/shard_map/cbm,db->dcm/dot_general | solution.py:47
  1007.8 11.8 fusion.50
  1047.6 20.8 %fusion.42 = (f32[1024,1024]{0,1:T(8,128)}, f32[1024,1024]{0,1:T(8,128)}) fusion(f32[1024,1024]{0,1:T(8,128)} %mul.725, f32[1,1024,1024]{1,2,0:T(8,128)} %copy.279, f32[1024,1027]{0,1:T(8,128)} %slice.174, f32[1024,1027]{0,1:T(8,128)} %slice.172, f32[1,1024,1024]{1,2,0:T(8,128)} %copy.278), kind=kLoop, calls=%fused_computation.90 | loop fusion | flops 25165824 | bytes 54525952 | tf_op jit(solution)/shard_map/mul | solution.py:240
  1077.2 9.8 slice.194
  1142.0 20.7 %add_bitcast_fusion.1 = (f32[1024,1024,1]{0,1,2:T(8,128)S(1)}, f32[1024,1024,1]{0,1,2:T(8,128)S(1)}) fusion(f32[1024,1024]{0,1:T(8,128)} %reshape.132, f32[1024,1024]{0,1:T(8,128)} %get-tuple-element.32, f32[1024,3]{0,1:T(4,128)S(1)} %get-tuple-element.57, f32[1024,3]{0,1:T(4,128)S(1)} %get-tuple-element.56), kind=kLoop, calls=%fused_computation.87 | loop fusion | flops 41943040 | bytes 16801792 | tf_op jit(solution)/shard_map/stack | solution.py:124
  1164.4 13.0 %copy.271 = f32[1024,1024,2]{0,2,1:T(2,128)} copy(f32[1024,1024,2]{0,1,2:T(8,128)S(1)} %pad_maximum_fusion.3) | data formatting | bytes 16777216 | tf_op jit(solution)/shard_map/stack | solution.py:124
  1177.4 11.0 reshape.133
  1205.9 13.6 %fusion.12 = f32[1024,2048]{0,1:T(8,128)} fusion(f32[1024,2048]{0,1:T(8,128)} %copy.272, f32[1024,2048]{0,1:T(8,128)} %reshape.133, f32[1024,8,256]{0,2,1:T(8,128)} %copy.265), kind=kLoop, calls=%fused_computation.33 | loop fusion | flops 8388608 | bytes 33554432 | tf_op jit(solution)/shard_map/max | solution.py:250
  (128 shorter events, 228.6 us)
Async XLA Ops:
  7.2 590.7 %copy-start = (f32[128,128]{1,0:T(8,128)S(1)}, f32[128,128]{1,0:T(8,128)}, u32[]{:S(2)}) copy-start(f32[128,128]{1,0:T(8,128)} %param.15) | copy-start | bytes 196612
  16.5 5.3 copy-start.17
  16.5 119.8 %all-to-all-start = ((f32[1024,8,256]{0,2,1:T(8,128)}), f32[1024,8,256]{0,2,1:T(8,128)}, u32[]{:S(2)}, u32[]{:S(2)}) async-start(f32[1024,8,256]{0,2,1:T(8,128)} %bitcast.124), calls=%async_computation | async-start | bytes 16777216 | tf_op jit(solution)/shard_map/all_to_all | solution.py:169
  92.8 0.7 copy-start.15
  93.0 69.9 %copy-start.8 = (f32[64,128]{0,1:T(8,128)}, f32[64,128]{0,1:T(8,128)S(1)}, u32[]{:S(2)}) copy-start(f32[64,128]{0,1:T(8,128)S(1)} %get-tuple-element.65) | copy-start | bytes 98308
  93.5 0.6 copy-start.10
  181.5 17.5 %slice-start.4 = ((s8[8388608]{0:T(1024)(128)(4,1)}), s8[4194304]{0:T(1024)(128)(4,1)S(1)}, s32[]{:S(2)}) async-start(s8[8388608]{0:T(1024)(128)(4,1)} %bitcast.129), calls=%async_computation.10 | async-start | bytes 8388608
  181.5 17.5 %slice-start.5 = ((s8[8388608]{0:T(1024)(128)(4,1)}), s8[4194304]{0:T(1024)(128)(4,1)S(1)}, s32[]{:S(2)}) async-start(s8[8388608]{0:T(1024)(128)(4,1)} %bitcast.129), calls=%async_computation.11 | async-start | bytes 8388608
  351.3 19.2 %copy-start.16 = (s32[256]{0:T(256)S(1)}, s32[256]{0:T(256)}, u32[]{:S(2)}) copy-start(s32[256]{0:T(256)} %copy-done.15) | copy-start | bytes 3076
  370.5 17.2 %copy-start.2 = (f32[8192,256]{0,1:T(8,128)S(1)}, f32[8192,256]{0,1:T(8,128)}, u32[]{:S(2)}) copy-start(f32[8192,256]{0,1:T(8,128)} %get-tuple-element.37) | copy-start | bytes 25165828
  387.8 29.4 %slice-start = ((s8[8388608]{0:T(1024)(128)(4,1)}), s8[4194304]{0:T(1024)(128)(4,1)S(1)}, s32[]{:S(2)}) async-start(s8[8388608]{0:T(1024)(128)(4,1)} %bitcast.122), calls=%async_computation.6 | async-start | bytes 8388608
  402.3 14.8 %slice-start.1 = ((s8[8388608]{0:T(1024)(128)(4,1)}), s8[4194304]{0:T(1024)(128)(4,1)S(1)}, s32[]{:S(2)}) async-start(s8[8388608]{0:T(1024)(128)(4,1)} %bitcast.122), calls=%async_computation.7 | async-start | bytes 8388608
  560.9 37.0 %copy-start.13 = (f32[256,2,128]{2,1,0:T(2,128)S(1)}, f32[256,2,128]{2,1,0:T(2,128)}, u32[]{:S(2)}) copy-start(f32[256,2,128]{2,1,0:T(2,128)} %param.14) | copy-start | bytes 786436
  560.9 37.0 %copy-start.14 = (f32[256,2,128]{2,1,0:T(2,128)S(1)}, f32[256,2,128]{2,1,0:T(2,128)}, u32[]{:S(2)}) copy-start(f32[256,2,128]{2,1,0:T(2,128)} %param.12) | copy-start | bytes 786436
  568.4 28.9 %all-to-all-start.2 = ((f32[1024,2,128]{2,1,0:T(2,128)}), f32[1024,2,128]{2,1,0:T(2,128)S(1)}, u32[]{:S(2)}, u32[]{:S(2)}) async-start(f32[1024,2,128]{2,1,0:T(2,128)} %reduce_sum.36), calls=%async_computation.2 | async-start | bytes 2097152 | tf_op jit(solution)/shard_map/all_to_all | solution.py:206
  571.9 97.1 %all-gather.4.cloned.1.call-start = ((), (), s32[]{:S(2)}) async-start(), calls=%async_computation.4 | async-start | bytes 1310720 | tf_op jit(solution)/shard_map/all_gather | solution.py:218
  637.8 0.7 copy-start.6
  639.6 136.3 %all-gather.6.cloned.1.call-start = ((), (), s32[]{:S(2)}) async-start(), calls=%async_computation.5 | async-start | bytes 9437184 | tf_op jit(solution)/shard_map/all_gather | solution.py:219
  669.0 11.3 slice-start.2
  670.0 10.4 slice-start.3
  670.0 10.4 collective-permute-start
  722.2 18.0 %copy-start.11 = (s32[8192]{0:T(1024)S(1)}, s32[8192]{0:T(1024)}, u32[]{:S(2)}) copy-start(s32[8192]{0:T(1024)} %copy-done.10) | copy-start | bytes 98308
  735.9 2.0 copy-start.5
  737.9 13.2 %collective-permute-start.1 = (f32[1024,6]{0,1:T(8,128)S(1)}, f32[1024,6]{0,1:T(8,128)S(1)}, u32[]{:S(2)}, u32[]{:S(2)}) collective-permute-start(f32[1024,6]{0,1:T(8,128)S(1)} %slice.235), channel_id=1, source_target_pairs={{1,0},{2,1},{3,2},{0,3},{5,4},{6,5},{7,6},{4,7},{9,8},{10,9},{11,1... | collective-permute-start | bytes 73736 | tf_op jit(solution)/shard_map/ppermute | solution.py:26
  776.0 10.0 copy-start.3
  956.8 13.2 %copy-start.9 = (f32[64,128]{0,1:T(8,128)S(1)}, f32[64,128]{0,1:T(8,128)}, u32[]{:S(2)}) copy-start(f32[64,128]{0,1:T(8,128)} %copy-done.8) | copy-start | bytes 98308
  956.8 13.2 %copy-start.12 = (f32[64,128]{0,1:T(8,128)S(1)}, f32[64,128]{0,1:T(8,128)}, u32[]{:S(2)}) copy-start(f32[64,128]{0,1:T(8,128)} %fusion.138) | copy-start | bytes 98308
  991.5 16.3 %slice-start.6 = ((s8[8388608]{0:T(1024)(128)(4,1)}), s8[4194304]{0:T(1024)(128)(4,1)S(1)}, s32[]{:S(2)}) async-start(s8[8388608]{0:T(1024)(128)(4,1)} %bitcast.140), calls=%async_computation.12 | async-start | bytes 8388608
  991.5 16.3 %slice-start.7 = ((s8[8388608]{0:T(1024)(128)(4,1)}), s8[4194304]{0:T(1024)(128)(4,1)S(1)}, s32[]{:S(2)}) async-start(s8[8388608]{0:T(1024)(128)(4,1)} %bitcast.140), calls=%async_computation.13 | async-start | bytes 8388608
  1027.9 5.1 copy-start.4
  1028.0 161.3 %all-to-all-start.3 = ((f32[8,1024,256]{2,1,0:T(8,128)}), f32[8,1024,256]{2,1,0:T(8,128)}, u32[]{:S(2)}, u32[]{:S(2)}) async-start(f32[8,1024,256]{2,1,0:T(8,128)} %bitcast.139), calls=%async_computation.3 | async-start | bytes 16777216 | tf_op jit(solution)/shard_map/all_to_all | solution.py:233
  1099.4 10.0 collective-permute-start.2
  1123.5 18.5 %collective-permute-start.3 = (f32[2,1024,3]{1,2,0:T(4,128)S(1)}, f32[2,1024,3]{1,2,0:T(4,128)S(1)}, u32[]{:S(2)}, u32[]{:S(2)}) collective-permute-start(f32[2,1024,3]{1,2,0:T(4,128)S(1)} %pad_maximum_fusion.11), channel_id=1, source_target_pairs={{3,0},{0,1},{1,2},{2,3},{7,4},{4,5},{5,6},{6,7},{11,8},{8,9},{9,10... | collective-permute-start | bytes 73736 | tf_op jit(solution)/shard_map/ppermute | solution.py:26
  1177.4 11.0 copy-start.7
  1205.9 22.8 %copy-start.1 = (f32[128,128]{1,0:T(8,128)S(1)}, f32[128,128]{1,0:T(8,128)}, u32[]{:S(2)}) copy-start(f32[128,128]{1,0:T(8,128)} %param.15) | copy-start | bytes 196612
Sparse Core Ops, SparseCore 0:
  639.8 29.2 all-gather.3
  670.9 53.6 all-gather.5
where the time goes:
time: 1250 us; the launch traced here: 1240 us
  local copies, waits for them, and re-layouts  373 us (30%)
  matrix products  355 us (28%)
  other arithmetic  212 us (17%)
  blocking collectives  206 us (16%)
  waiting for transfers between devices  53.5 us (4%)
  starting transfers between devices  19 us (2%)
  between operations  17 us (1%)
    all_to_all x1, blocking collectives, on_device(): lax.all_to_all(partial, 'vis', split_axis=0, concat_axis=0, tiled=True)  97.4 us
    all_gather x1, blocking collectives, on_device(): all_index = lax.all_gather(block_index, ('vis', 'tile'), tiled=True)  70.9 us
    dot_general x4, matrix products, complex_einsum(): real_part = jnp.einsum(form, left_real, table_cos, precision=precise)  68.3 us
    slice x4, local copies, waits for them, and re-layouts, analyse_local(): lax.slice_in_dim(extended, parity, extended.shape[1], 2, 1)  57.8 us
    unnamed x59, local copies, waits for them, and re-layouts  51.8 us
    dot_general x3, matrix products, complex_einsum(): imag_part = jnp.einsum(form, left_real, table_sin, precision=precise)  46 us
    gather x2, local copies, waits for them, and re-layouts, on_device(): picked_imag = jnp.take(spec_imag, row_of, axis=0)  43.6 us
    gather x2, local copies, waits for them, and re-layouts, on_device(): picked_real = jnp.take(spec_real, row_of, axis=0)  43.6 us
  transfers between devices with their start and end apart: 9, of which 2 were waited for; matrix products, arithmetic and copies ran while one was open for 24% of the time, Pallas kernels for 0%

commit v1 on v0

--- a/solution.py
+++ b/solution.py
@@ -168,7 +168,23 @@
     norm_scale = 1.0 / math.sqrt(len_rows * len_cols)
     columns = lax.all_to_all(extrapolated, "vis", split_axis=1, concat_axis=0, tiled=True)
     spec_real, spec_imag = transform_axis(columns, None, -1.0, 0, False)
-    all_index = lax.all_gather(block_index, ("vis", "tile"), tiled=True)
+    block_next = lax.axis_size(("vis", "tile"))
+    a_now, tmp, s_next = (block_next, lax.axis_index(("vis", "tile")), block_index.shape[0])
+    main, front = (block_index, 1)
+    while front < a_now:
+        main = jnp.concatenate(
+            [
+                main,
+                lax.ppermute(
+                    main,
+                    axis_name=("vis", "tile"),
+                    perm=[(it, (it - front) % a_now) for it in range(a_now)],
+                ),
+            ],
+            axis=0,
+        )
+        front = 2 * front
+    all_index = jnp.roll(main, tmp * s_next, axis=0)
     total_blocks = all_index.shape[0]
     owner = jnp.arange(total_blocks, dtype=jnp.int32) // slot_count
     per_row = slab_cols // block_width

time: 1250 us -> 1290 us (1.032)
  waiting for transfers between devices: 53.5 us -> 145 us
  blocking collectives: 206 us -> 136 us
    ppermute x0 -> x5, waiting for transfers between devices: none -> 91.9 us  [on_device(): lax.ppermute(main, axis_name=('vis', 'tile'), perm=[(it, (it - front) % a...]
    all_gather x1 -> x0, blocking collectives: 70.9 us -> none  [on_device(): all_index = lax.all_gather(block_index, ('vis', 'tile'), tiled=True)]
    unnamed x59 -> x69, local copies, waits for them, and re-layouts: 51.8 us -> 52.4 us
  transfers between devices with their start and end apart: 9 -> 14, of which waited for: 2 -> 6; matrix products, arithmetic and copies ran while one was open for 24% -> 24% of each run, Pallas kernels for 0% -> 0%
where the time goes in v1:
time: 1290 us; the launch traced here: 1270 us
  local copies, waits for them, and re-layouts  374 us (29%)
  matrix products  355 us (28%)
  other arithmetic  213 us (17%)
  waiting for transfers between devices  145 us (11%)
  blocking collectives  136 us (11%)
  starting transfers between devices  30.6 us (2%)
  between operations  17.1 us (1%)
    all_to_all x1, blocking collectives, on_device(): lax.all_to_all(partial, 'vis', split_axis=0, concat_axis=0, tiled=True)  98.3 us
    ppermute x5, waiting for transfers between devices, on_device(): lax.ppermute(main, axis_name=('vis', 'tile'), perm=[(it, (it - front) % a...  91.9 us
    dot_general x4, matrix products, complex_einsum(): real_part = jnp.einsum(form, left_real, table_cos, precision=precise)  68.4 us
    slice x4, local copies, waits for them, and re-layouts, analyse_local(): lax.slice_in_dim(extended, parity, extended.shape[1], 2, 1)  58.1 us
    unnamed x69, local copies, waits for them, and re-layouts  52.4 us
    dot_general x3, matrix products, complex_einsum(): imag_part = jnp.einsum(form, left_real, table_sin, precision=precise)  46 us
    gather x2, local copies, waits for them, and re-layouts, on_device(): picked_real = jnp.take(spec_real, row_of, axis=0)  43.9 us
    gather x2, local copies, waits for them, and re-layouts, on_device(): picked_imag = jnp.take(spec_imag, row_of, axis=0)  43.8 us
  transfers between devices with their start and end apart: 14, of which 6 were waited for; matrix products, arithmetic and copies ran while one was open for 24% of the time, Pallas kernels for 0%

profile of v1, /device:TPU:0, one launch (start us, length us, event | category | flops | bytes accessed | tf_op | source)
XLA Modules:
  0.0 1271.4 jit_solution(12820349280067109435)
XLA Ops:
  35.0 84.1 %collective-permute-done.2 = s32[1024]{0:T(1024)S(1)} collective-permute-done((s32[1024]{0:T(1024)S(1)}, s32[1024]{0:T(1024)S(1)}, u32[]{:S(2)}, u32[]{:S(2)}) %collective-permute-start.2) | collective-permute-done | bytes 4128 | tf_op jit(solution)/shard_map/ppermute | solution.py:178
  127.6 19.4 %fusion.63 = f32[8192,1536]{0,1:T(8,128)} fusion(s32[8192]{0:T(1024)S(1)} %get-tuple-element.77, bf16[64,512]{1,0:T(8,128)(2,1)S(1)} %get-tuple-element.56, bf16[64,512]{1,0:T(8,128)(2,1)S(1)} %get-tuple-element.55, bf16[64,512]{1,0:T(8,128)(2,1)S(1)} %get-tuple-element.54), kind=kOutput, calls=%fused_computation.120 | convolution fusion | flops 1611726848 | bytes 50561024 | tf_op jit(solution)/shard_map/dot_general | solution.py:141
  147.0 22.7 %slice_add_fusion.2 = f32[8192,512]{0,1:T(8,128)} fusion(f32[8192,1536]{0,1:T(8,128)} %fusion.63), kind=kLoop, calls=%fused_computation.16 | loop fusion | flops 8388608 | bytes 67108864 | tf_op jit(solution)/shard_map/add | solution.py:142
  178.8 17.6 %fusion.33 = f32[64,128,256]{2,0,1:T(8,128)} fusion(f32[64,128,256]{2,1,0:T(8,128)} %bitcast.125), kind=kOutput, calls=%fused_computation.66 | convolution fusion | flops 1610670080 | bytes 16777216 | tf_op jit(solution)/shard_map/abm,ca->cbm/dot_general | solution.py:45
  196.4 18.5 %multiply_subtract_fusion.3 = (f32[64,128,256]{2,0,1:T(8,128)S(1)}, f32[64,128,256]{2,0,1:T(8,128)}) fusion(f32[64,128,256]{2,0,1:T(8,128)} %fusion.33, f32[64,128]{0,1:T(8,128)S(1)} %get-tuple-element.75, f32[64,128]{0,1:T(8,128)S(1)} %get-tuple-element.76, f32[64,128,256]{2,1,0:T(8,128)} %bitcast.126), kind=kOutput, calls=%fused_computation.48 | convolution fusion | flops 1627451392 | bytes 33619968 | tf_op jit(solution)/shard_map/abm,ca->cbm/dot_general | solution.py:50
  215.0 17.5 %fusion.27 = f32[128,64,256]{2,0,1:T(8,128)} fusion(f32[64,128,256]{2,0,1:T(8,128)} %get-tuple-element.42), kind=kOutput, calls=%fused_computation.60 | convolution fusion | flops 3221454848 | bytes 16777216 | tf_op jit(solution)/shard_map/cbm,db->dcm/dot_general | solution.py:52
  232.5 13.5 %fusion.25 = f32[128,64,256]{2,0,1:T(8,128)} fusion(f32[64,128,256]{2,0,1:T(8,128)S(1)} %bitcast.128), kind=kOutput, calls=%fused_computation.58 | convolution fusion | flops 3221471232 | bytes 16777216 | tf_op jit(solution)/shard_map/cbm,db->dcm/dot_general | solution.py:47
  246.1 14.3 %fusion.45 = f32[128,64,256]{2,0,1:T(8,128)S(1)} fusion(f32[128,64,256]{2,0,1:T(8,128)} %fusion.27, f32[64,128,256]{2,0,1:T(8,128)S(1)} %get-tuple-element.41), kind=kOutput, calls=%fused_computation.94 | convolution fusion | flops 3223568384 | bytes 25165824 | tf_op jit(solution)/shard_map/cbm,db->dcm/dot_general | solution.py:50
  268.6 17.4 %subtract_add_fusion.1 = f32[128,64,256]{2,0,1:T(8,128)} fusion(f32[128,64,256]{2,0,1:T(8,128)} %fusion.25, f32[128,64,256]{2,0,1:T(8,128)S(1)} %fusion.45, f32[64,128,256]{2,0,1:T(8,128)S(1)} %get-tuple-element.41), kind=kOutput, calls=%fused_computation.46 | convolution fusion | flops 3227746304 | bytes 33554432 | tf_op jit(solution)/shard_map/cbm,db->dcm/dot_general | solution.py:45
  286.1 11.5 copy.247
  297.6 34.9 %gather_fusion = f32[8192,256]{1,0:T(8,128)} fusion(f32[8192,256]{1,0:T(8,128)} %bitcast.119, s32[8192]{0:T(1024)S(1)} %get-tuple-element.78), kind=kCustom, calls=%fused_computation.clone | custom fusion | bytes 16809984 | tf_op jit(solution)/shard_map/jit(_take)/gather | solution.py:209
  341.5 34.9 %gather_fusion.1 = f32[8192,256]{1,0:T(8,128)} fusion(f32[8192,256]{1,0:T(8,128)} %bitcast.118, s32[8192]{0:T(1024)S(1)} %get-tuple-element.78), kind=kCustom, calls=%fused_computation.1.clone | custom fusion | bytes 16809984 | tf_op jit(solution)/shard_map/jit(_take)/gather | solution.py:210
  385.3 19.3 %multiply_add_fusion.2 = (f32[8192,256]{0,1:T(8,128)}, f32[8192,256]{0,1:T(8,128)}) fusion(f32[8192,256]{0,1:T(8,128)} %copy.250, f32[8192,256]{0,1:T(8,128)} %copy.248, f32[8192,512]{0,1:T(8,128)} %slice_add_fusion.2, pred[8192]{0:T(1024)(128)(4,1)S(1)} %get-tuple-element.30), kind=kLoop, calls=%fused_computation.45 | loop fusion | flops 16777216 | bytes 50339840 | tf_op jit(solution)/shard_map/add | solution.py:211
  404.6 17.2 %fusion.104 = f32[8192,128]{1,0:T(8,128)S(1)} fusion(f32[8192,256]{0,1:T(8,128)} %get-tuple-element.37, s32[256]{0:T(256)S(1)} %copy-done.16), kind=kOutput, calls=%fused_computation.183 | convolution fusion | flops 3221684224 | bytes 12583936 | tf_op jit(solution)/shard_map/dot_general | solution.py:213
  421.9 14.6 %fusion.102 = f32[8192,128]{1,0:T(8,128)S(1)} fusion(f32[8192,256]{0,1:T(8,128)S(1)} %copy-done.2, s32[256]{0:T(256)S(1)} %copy-done.16), kind=kOutput, calls=%fused_computation.182 | convolution fusion | flops 3221684224 | bytes 12583936 | tf_op jit(solution)/shard_map/dot_general | solution.py:216
  436.5 14.8 %fusion.9 = f32[8192,1,128]{2,0,1:T(8,128)S(1)} fusion(f32[8192,128]{1,0:T(8,128)S(1)} %fusion.104, f32[8192,256]{0,1:T(8,128)S(1)} %copy-done.2, s32[256]{0:T(256)S(1)} %copy-done.16), kind=kOutput, calls=%fused_computation.25 | convolution fusion | flops 3222732800 | bytes 16778240 | tf_op jit(solution)/shard_map/dot_general | solution.py:213
  451.3 14.6 %fusion.8 = f32[8192,1,128]{2,0,1:T(8,128)S(1)} fusion(f32[8192,128]{1,0:T(8,128)S(1)} %fusion.102, f32[8192,256]{0,1:T(8,128)S(1)} %bitcast.121, s32[256]{0:T(256)S(1)} %copy-done.16), kind=kOutput, calls=%fused_computation.23 | convolution fusion | flops 3222732800 | bytes 16778240 | tf_op jit(solution)/shard_map/dot_general | solution.py:216
  466.4 31.2 %copy.251 = f32[8192,2,128]{2,1,0:T(2,128)S(1)} copy(f32[8192,2,128]{2,0,1:T(8,128)S(1)} %pad_maximum_fusion.2) | data formatting | bytes 16777216 | tf_op jit(solution)/shard_map/stack | solution.py:219
  497.6 98.3 %all_to_all.39 = f32[8192,2,128]{2,1,0:T(2,128)} all-to-all(f32[8192,2,128]{2,1,0:T(2,128)S(1)} %copy.251), channel_id=1, replica_groups=mesh['vis'=8,'tile'=4] {'vis'}, dimensions={0} | all-to-all | bytes 16777216 | tf_op jit(solution)/shard_map/all_to_all | solution.py:220
  608.2 24.1 %all-to-all-done.2 = f32[1024,2,128]{2,1,0:T(2,128)S(1)} async-done(((f32[1024,2,128]{2,1,0:T(2,128)}), f32[1024,2,128]{2,1,0:T(2,128)S(1)}, u32[]{:S(2)}, u32[]{:S(2)}) %all-to-all-start.2) | async-done | bytes 1048608 | tf_op jit(solution)/shard_map/all_to_all | solution.py:222
  633.9 37.5 %all-reduce = (f32[]{:T(128)}, f32[]{:T(128)}) all-reduce(f32[]{:T(128)} %fusion.168, f32[]{:T(128)} %get-tuple-element.71), channel_id=1, replica_groups=mesh['vis'=8,'tile'=4] {'vis','tile'}, use_global_device_ids=true, to_apply=%region_3.5 | all-reduce | flops 2 | bytes 16 | tf_op jit(solution)/shard_map/psum | solution.py:229
  674.7 29.3 %all-gather.3.cloned.1.call-done = f32[1024,2,128]{2,0,1:T(8,128)} async-done(((f32[256,2,128]{2,0,1:T(8,128)}), f32[1024,2,128]{2,0,1:T(8,128)}) %all-gather.3.cloned.1.call-update) | async-done | bytes 1048592 | tf_op jit(solution)/shard_map/all_gather | solution.py:234
  719.5 19.0 %slice.172 = f32[1024,1027]{0,1:T(8,128)} slice(f32[1024,2054]{0,1:T(8,128)} %pad_maximum_fusion.1), slice={[0:1024:1], [0:2054:2]} | slice | bytes 8413184 | tf_op jit(solution)/shard_map/slice | solution.py:100
  738.5 19.0 %slice.174 = f32[1024,1027]{0,1:T(8,128)} slice(f32[1024,2054]{0,1:T(8,128)} %pad_maximum_fusion.1), slice={[0:1024:1], [1:2054:2]} | slice | bytes 8413184 | tf_op jit(solution)/shard_map/slice | solution.py:100
  757.5 13.5 %multiply_add_fusion.5 = f32[1024,1024]{0,1:T(8,128)S(1)} fusion(f32[1024,1027]{0,1:T(8,128)} %slice.174, f32[1024,1027]{0,1:T(8,128)} %slice.172), kind=kLoop, calls=%fused_computation.91 | loop fusion | flops 15728640 | bytes 37748736 | tf_op jit(solution)/shard_map/add | solution.py:107
  791.0 10.1 slice.184
  801.1 10.1 slice.186
  811.1 10.0 fusion.44
  821.2 10.1 fusion.43
  831.2 10.6 convolution_subtract_fusion
  841.8 22.0 %multiply_subtract_fusion.1 = (f32[8192,256]{0,1:T(8,128)}, f32[8192,256]{0,1:T(8,128)}) fusion(f32[8192,256]{0,1:T(8,128)} %convolution_subtract_fusion, f32[8192,512]{0,1:T(8,128)} %slice_add_fusion.2, f32[8192,256]{0,1:T(8,128)} %fusion.43, s32[256]{0:T(256)S(1)} %copy-done.16, f32[8192,2,128]{2,0,1:T(8,128)} %all-gather.5.cloned.1.call-done), kind=kOutput, calls=%fused_computation.43 | convolution fusion | flops 3236364288 | bytes 54526976 | tf_op jit(solution)/shard_map/dot_general | solution.py:239
  863.8 11.7 pad_maximum_fusion
  875.5 17.5 %copy.276 = f32[8192,512]{1,0:T(8,128)} copy(f32[8192,512]{0,1:T(8,128)} %pad_maximum_fusion) | data formatting | bytes 33554432 | tf_op jit(solution)/shard_map/reshape | solution.py:245
  893.0 10.4 reduce-precision_convert_fusion.1
  903.4 31.6 %fusion = f32[8,1024,1536]{2,1,0:T(8,128)} fusion(bf16[8,1024,512]{2,1,0:T(8,128)(2,1)S(1)} %get-tuple-element.46, bf16[8,1024,512]{2,1,0:T(8,128)(2,1)} %get-tuple-element.47, bf16[8,1024,512]{2,1,0:T(8,128)(2,1)S(1)} %get-tuple-element.45, s32[8,1024]{1,0:T(8,128)S(1)} %eq.48), kind=kOutput, calls=%fused_computation.3 | convolution fusion | flops 25853689856 | bytes 75530240 | tf_op jit(solution)/shard_map/gkb,gbc->gkc/dot_general | solution.py:151
  934.9 23.9 %slice_add_fusion = f32[8,1024,512]{2,1,0:T(8,128)} fusion(f32[8,1024,1536]{2,1,0:T(8,128)} %fusion), kind=kLoop, calls=%fused_computation.14 | loop fusion | flops 8388608 | bytes 67108864 | tf_op jit(solution)/shard_map/add | solution.py:152
  965.2 13.2 %fusion.17 = f32[64,128,256]{2,0,1:T(8,128)} fusion(f32[64,128,256]{2,1,0:T(8,128)S(1)} %bitcast.129), kind=kOutput, calls=%fused_computation.50 | convolution fusion | flops 1610670080 | bytes 16777216 | tf_op jit(solution)/shard_map/abm,ca->cbm/dot_general | solution.py:47
  978.4 13.6 %fusion.19 = f32[64,128,256]{2,0,1:T(8,128)} fusion(f32[64,128,256]{2,1,0:T(8,128)S(1)} %bitcast.130), kind=kOutput, calls=%fused_computation.52 | convolution fusion | flops 1610670080 | bytes 16777216 | tf_op jit(solution)/shard_map/abm,ca->cbm/dot_general | solution.py:52
  992.0 13.2 %fusion.23 = f32[64,128,256]{2,0,1:T(8,128)} fusion(f32[64,128,256]{2,1,0:T(8,128)S(1)} %bitcast.131), kind=kOutput, calls=%fused_computation.56 | convolution fusion | flops 1610670080 | bytes 16777216 | tf_op jit(solution)/shard_map/abm,ca->cbm/dot_general | solution.py:50
  1005.2 21.5 %multiply_subtract_fusion = (f32[64,128,256]{2,0,1:T(8,128)}, f32[64,128,256]{2,0,1:T(8,128)}) fusion(f32[64,128,256]{2,0,1:T(8,128)} %fusion.17, f32[64,128]{0,1:T(8,128)S(1)} %copy-done.12, f32[64,128]{0,1:T(8,128)S(1)} %copy-done.9, f32[64,128,256]{2,0,1:T(8,128)} %fusion.23, f32[64,128,256]{2,0,1:T(8,128)} %fusion.19, f32[64,128,256]{2,1,0:T(8,128)S(1)} %bitcast.132), kind=kOutput, calls=%fused_computation.40 | convolution fusion | flops 1631641600 | bytes 50397184 | tf_op jit(solution)/shard_map/abm,ca->cbm/dot_general | solution.py:45
  1026.8 16.3 %fusion.13 = f32[128,64,256]{2,0,1:T(8,128)S(1)} fusion(f32[64,128,256]{2,0,1:T(8,128)} %get-tuple-element.36), kind=kOutput, calls=%fused_computation.34 | convolution fusion | flops 3221454848 | bytes 16777216 | tf_op jit(solution)/shard_map/cbm,db->dcm/dot_general | solution.py:47
  1043.1 11.8 fusion.50
  1082.9 20.8 %fusion.42 = (f32[1024,1024]{0,1:T(8,128)}, f32[1024,1024]{0,1:T(8,128)}) fusion(f32[1024,1024]{0,1:T(8,128)} %mul.733, f32[1,1024,1024]{1,2,0:T(8,128)} %copy.279, f32[1024,1027]{0,1:T(8,128)} %slice.174, f32[1024,1027]{0,1:T(8,128)} %slice.172, f32[1,1024,1024]{1,2,0:T(8,128)} %copy.278), kind=kLoop, calls=%fused_computation.90 | loop fusion | flops 25165824 | bytes 54525952 | tf_op jit(solution)/shard_map/mul | solution.py:256
  1122.4 9.8 slice.195
  1177.4 20.8 %add_bitcast_fusion.1 = (f32[1024,1024,1]{0,1,2:T(8,128)S(1)}, f32[1024,1024,1]{0,1,2:T(8,128)S(1)}) fusion(f32[1024,1024]{0,1:T(8,128)} %reshape.132, f32[1024,1024]{0,1:T(8,128)} %get-tuple-element.33, f32[1024,3]{0,1:T(4,128)S(1)} %get-tuple-element.58, f32[1024,3]{0,1:T(4,128)S(1)} %get-tuple-element.57), kind=kLoop, calls=%fused_computation.87 | loop fusion | flops 41943040 | bytes 16801792 | tf_op jit(solution)/shard_map/stack | solution.py:124
  1199.9 13.0 %copy.271 = f32[1024,1024,2]{0,2,1:T(2,128)} copy(f32[1024,1024,2]{0,1,2:T(8,128)S(1)} %pad_maximum_fusion.3) | data formatting | bytes 16777216 | tf_op jit(solution)/shard_map/stack | solution.py:124
  1212.8 11.0 reshape.133
  1241.4 13.6 %fusion.12 = f32[1024,2048]{0,1:T(8,128)} fusion(f32[1024,2048]{0,1:T(8,128)} %copy.272, f32[1024,2048]{0,1:T(8,128)} %reshape.133, f32[1024,8,256]{0,2,1:T(8,128)} %copy.265), kind=kLoop, calls=%fused_computation.33 | loop fusion | flops 8388608 | bytes 33554432 | tf_op jit(solution)/shard_map/max | solution.py:266
  (153 shorter events, 249.1 us)
Async XLA Ops:
  7.2 625.7 %copy-start = (f32[128,128]{1,0:T(8,128)S(1)}, f32[128,128]{1,0:T(8,128)}, u32[]{:S(2)}) copy-start(f32[128,128]{1,0:T(8,128)} %param.15) | copy-start | bytes 196612
  7.2 21.8 %collective-permute-start = (s32[256]{0:T(256)}, s32[256]{0:T(256)S(1)}, u32[]{:S(2)}, u32[]{:S(2)}) collective-permute-start(s32[256]{0:T(256)} %param.16), channel_id=1, source_target_pairs={{0,31},{1,0},{2,1},{3,2},{4,3},{5,4},{6,5},{7,6},{8,7},{9,8},{10,9... | collective-permute-start | bytes 3080 | tf_op jit(solution)/shard_map/ppermute | solution.py:178
  22.9 6.1 copy-start.17
  22.9 146.8 %all-to-all-start = ((f32[1024,8,256]{0,2,1:T(8,128)}), f32[1024,8,256]{0,2,1:T(8,128)}, u32[]{:S(2)}, u32[]{:S(2)}) async-start(f32[1024,8,256]{0,2,1:T(8,128)} %bitcast.122), calls=%async_computation | async-start | bytes 16777216 | tf_op jit(solution)/shard_map/all_to_all | solution.py:169
  28.0 0.6 copy-start.15
  29.1 4.5 collective-permute-start.1
  33.6 85.5 %collective-permute-start.2 = (s32[1024]{0:T(1024)S(1)}, s32[1024]{0:T(1024)S(1)}, u32[]{:S(2)}, u32[]{:S(2)}) collective-permute-start(s32[1024]{0:T(1024)S(1)} %pad_add_fusion.1), channel_id=1, source_target_pairs={{0,28},{1,29},{2,30},{3,31},{4,0},{5,1},{6,2},{7,3},{8,4},{9,5},{1... | collective-permute-start | bytes 12296 | tf_op jit(solution)/shard_map/ppermute | solution.py:178
  119.1 3.9 collective-permute-start.3
  123.0 3.8 collective-permute-start.4
  124.7 71.8 %copy-start.8 = (f32[64,128]{0,1:T(8,128)}, f32[64,128]{0,1:T(8,128)S(1)}, u32[]{:S(2)}) copy-start(f32[64,128]{0,1:T(8,128)S(1)} %get-tuple-element.76) | copy-start | bytes 98308
  126.9 0.6 copy-start.10
  215.0 17.5 %slice-start.4 = ((s8[8388608]{0:T(1024)(128)(4,1)}), s8[4194304]{0:T(1024)(128)(4,1)S(1)}, s32[]{:S(2)}) async-start(s8[8388608]{0:T(1024)(128)(4,1)} %bitcast.127), calls=%async_computation.10 | async-start | bytes 8388608
  215.0 17.6 %slice-start.5 = ((s8[8388608]{0:T(1024)(128)(4,1)}), s8[4194304]{0:T(1024)(128)(4,1)S(1)}, s32[]{:S(2)}) async-start(s8[8388608]{0:T(1024)(128)(4,1)} %bitcast.127), calls=%async_computation.11 | async-start | bytes 8388608
  385.3 19.3 %copy-start.16 = (s32[256]{0:T(256)S(1)}, s32[256]{0:T(256)}, u32[]{:S(2)}) copy-start(s32[256]{0:T(256)} %copy-done.15) | copy-start | bytes 3076
  404.6 17.2 %copy-start.2 = (f32[8192,256]{0,1:T(8,128)S(1)}, f32[8192,256]{0,1:T(8,128)}, u32[]{:S(2)}) copy-start(f32[8192,256]{0,1:T(8,128)} %get-tuple-element.38) | copy-start | bytes 25165828
  421.9 29.4 %slice-start = ((s8[8388608]{0:T(1024)(128)(4,1)}), s8[4194304]{0:T(1024)(128)(4,1)S(1)}, s32[]{:S(2)}) async-start(s8[8388608]{0:T(1024)(128)(4,1)} %bitcast.120), calls=%async_computation.6 | async-start | bytes 8388608
  436.4 14.8 %slice-start.1 = ((s8[8388608]{0:T(1024)(128)(4,1)}), s8[4194304]{0:T(1024)(128)(4,1)S(1)}, s32[]{:S(2)}) async-start(s8[8388608]{0:T(1024)(128)(4,1)} %bitcast.120), calls=%async_computation.7 | async-start | bytes 8388608
  595.9 37.0 %copy-start.13 = (f32[256,2,128]{2,1,0:T(2,128)S(1)}, f32[256,2,128]{2,1,0:T(2,128)}, u32[]{:S(2)}) copy-start(f32[256,2,128]{2,1,0:T(2,128)} %param.14) | copy-start | bytes 786436
  595.9 37.0 %copy-start.14 = (f32[256,2,128]{2,1,0:T(2,128)S(1)}, f32[256,2,128]{2,1,0:T(2,128)}, u32[]{:S(2)}) copy-start(f32[256,2,128]{2,1,0:T(2,128)} %param.12) | copy-start | bytes 786436
  603.3 28.9 %all-to-all-start.2 = ((f32[1024,2,128]{2,1,0:T(2,128)}), f32[1024,2,128]{2,1,0:T(2,128)S(1)}, u32[]{:S(2)}, u32[]{:S(2)}) async-start(f32[1024,2,128]{2,1,0:T(2,128)} %reduce_sum.36), calls=%async_computation.2 | async-start | bytes 2097152 | tf_op jit(solution)/shard_map/all_to_all | solution.py:222
  606.9 97.1 %all-gather.3.cloned.1.call-start = ((), (), s32[]{:S(2)}) async-start(), calls=%async_computation.4 | async-start | bytes 1310720 | tf_op jit(solution)/shard_map/all_gather | solution.py:234
  672.8 0.7 copy-start.6
  674.6 136.5 %all-gather.5.cloned.1.call-start = ((), (), s32[]{:S(2)}) async-start(), calls=%async_computation.5 | async-start | bytes 9437184 | tf_op jit(solution)/shard_map/all_gather | solution.py:235
  704.0 11.3 slice-start.2
  705.0 10.4 slice-start.3
  705.0 10.4 collective-permute-start.5
  771.0 2.0 copy-start.5
  773.0 13.1 %collective-permute-start.6 = (f32[1024,6]{0,1:T(8,128)S(1)}, f32[1024,6]{0,1:T(8,128)S(1)}, u32[]{:S(2)}, u32[]{:S(2)}) collective-permute-start(f32[1024,6]{0,1:T(8,128)S(1)} %slice.235), channel_id=1, source_target_pairs={{1,0},{2,1},{3,2},{0,3},{5,4},{6,5},{7,6},{4,7},{9,8},{10,9},{11,1... | collective-permute-start | bytes 73736 | tf_op jit(solution)/shard_map/ppermute | solution.py:26
  780.8 5.4 copy-start.11
  811.1 10.0 copy-start.3
  992.0 13.2 %copy-start.9 = (f32[64,128]{0,1:T(8,128)S(1)}, f32[64,128]{0,1:T(8,128)}, u32[]{:S(2)}) copy-start(f32[64,128]{0,1:T(8,128)} %copy-done.8) | copy-start | bytes 98308
  992.0 13.2 %copy-start.12 = (f32[64,128]{0,1:T(8,128)S(1)}, f32[64,128]{0,1:T(8,128)}, u32[]{:S(2)}) copy-start(f32[64,128]{0,1:T(8,128)} %fusion.138) | copy-start | bytes 98308
  1026.7 16.3 %slice-start.6 = ((s8[8388608]{0:T(1024)(128)(4,1)}), s8[4194304]{0:T(1024)(128)(4,1)S(1)}, s32[]{:S(2)}) async-start(s8[8388608]{0:T(1024)(128)(4,1)} %bitcast.138), calls=%async_computation.12 | async-start | bytes 8388608
  1026.8 16.3 %slice-start.7 = ((s8[8388608]{0:T(1024)(128)(4,1)}), s8[4194304]{0:T(1024)(128)(4,1)S(1)}, s32[]{:S(2)}) async-start(s8[8388608]{0:T(1024)(128)(4,1)} %bitcast.138), calls=%async_computation.13 | async-start | bytes 8388608
  1063.3 5.1 copy-start.4
  1063.3 161.5 %all-to-all-start.3 = ((f32[8,1024,256]{2,1,0:T(8,128)}), f32[8,1024,256]{2,1,0:T(8,128)}, u32[]{:S(2)}, u32[]{:S(2)}) async-start(f32[8,1024,256]{2,1,0:T(8,128)} %bitcast.137), calls=%async_computation.3 | async-start | bytes 16777216 | tf_op jit(solution)/shard_map/all_to_all | solution.py:249
  1134.8 10.1 collective-permute-start.7
  1159.0 18.3 %collective-permute-start.8 = (f32[2,1024,3]{1,2,0:T(4,128)S(1)}, f32[2,1024,3]{1,2,0:T(4,128)S(1)}, u32[]{:S(2)}, u32[]{:S(2)}) collective-permute-start(f32[2,1024,3]{1,2,0:T(4,128)S(1)} %pad_maximum_fusion.11), channel_id=1, source_target_pairs={{3,0},{0,1},{1,2},{2,3},{7,4},{4,5},{5,6},{6,7},{11,8},{8,9},{9,10... | collective-permute-start | bytes 73736 | tf_op jit(solution)/shard_map/ppermute | solution.py:26
  1212.8 11.0 copy-start.7
  1241.4 22.8 %copy-start.1 = (f32[128,128]{1,0:T(8,128)S(1)}, f32[128,128]{1,0:T(8,128)}, u32[]{:S(2)}) copy-start(f32[128,128]{1,0:T(8,128)} %param.15) | copy-start | bytes 196612
Sparse Core Ops, SparseCore 0:
  674.7 29.2 all-gather.2
  705.9 53.6 all-gather.4
